TPU v7x, 512 devices: a whole 4x8x8 slice. The times are simulated.
512 devices in a mesh: dp: 16 (over y, core), cell: 32 (over x, z).
Axes of the slice: x: 4, y: 8, z: 8, core: 2. Of those that a mesh axis runs over, the one named last changes fastest.
Arguments:
- sensitivity: bfloat16 [2048, 200704], P('dp', 'cell'), may hold values from -0.0390625 to 0.0390625
- direction: bfloat16 [16, 200704], P(None, 'cell'), may hold values from -6 to 6
- depth_weight: float32 [200704], P('cell'), may hold values from 0.3 to 3
- counts: int32 [32], P('cell'), may hold values from 4704 to 6272, as said below
- send_lists: int32 [32, 2, 128], P('cell'), may hold values from 0 to 6271, as said below
- neighbours: int32 [6, 200704], P(None, 'cell'), may hold values from 0 to 6528, as said below
Outputs:
- product: float32 [16, 200704], P(None, 'cell')
Inputs may be any that keep to these rules, and one draw needn't show every extreme that they name: `counts`: every partition has at least 4704 live cells; some partition is full in every draw. `send_lists`: entries are local indices of live cells of their own partition. `neighbours`: entries below 6272 are live local cells that differ from the cell's own local index by at most 64; 6272 to 6527 name received rim cells; 6528 is an absent face; padded slots hold only absent faces.
All inputs are finite; a program needn't handle non-finite values.
Results may differ from a plain program's by a relative error of at most 0.0008.
Values sent between devices are 32-bit elements; how exact they have to be, the bound alone decides.
No kernel may reach another device: no remote copies, remote signals or barrier semaphores. Data moves between devices by JAX's collectives and lax.ppermute only.
A program may use at most 64 MiB of HBM per device.

v0:
```python
import jax
import jax.numpy as jnp
from jax import lax
from jax.sharding import PartitionSpec as P


def padded_2(value, sides, width):
    for axis, dim in sides:
        count, length = (lax.axis_size(axis), value.shape[dim])
        up = [(i, (i + 1) % count) for i in range(count - 1)]
        down = [(j, i) for i, j in up]
        last = lax.slice_in_dim(value, length - width, length, axis=dim)
        leading = lax.slice_in_dim(value, 0, width, axis=dim)
        before = lax.ppermute(last, axis, up)
        after = lax.ppermute(leading, axis, down)
        value = jnp.concatenate([before, value, after], axis=dim)
    return value


def pick_block():
    block_len = 8
    for candidate in range(128, 7, -8):
        block_len = candidate
        break
    return block_len


def pick_group(block_count):
    group_len = 1
    for candidate in range(1, 9):
        if block_count % candidate == 0:
            group_len = candidate
    return group_len


def smoothness(masked_f, weight, send_lists, neighbours, width):
    slots = masked_f.shape[1]
    values = jnp.concatenate([masked_f * weight[None, :], weight[None, :]], axis=0)
    picked = jnp.take(values, send_lists[0].reshape(-1), axis=1)
    rim = picked.shape[1] // 2
    padded = padded_2(picked, (("cell", 1),), rim)
    rim_vals = jnp.concatenate([padded[:, :rim], padded[:, 3 * rim :]], axis=1)
    lanes = values.shape[0]
    block_len = pick_block()
    block_count = width // block_len
    pieces = 1 + (128 + block_len - 1) // block_len
    spread = jnp.pad(values, ((0, 0), (64, pieces * block_len)))
    local_vals = lax.slice_in_dim(spread, 0, (block_count + pieces - 1) * block_len, axis=1)
    shifted = [
        local_vals[:, m * block_len : (m + block_count) * block_len].reshape(
            lanes, block_count, block_len
        )
        for m in range(pieces)
    ]
    rim_part = jnp.broadcast_to(rim_vals[:, None, :], (lanes, block_count, 2 * rim))
    windows = jnp.concatenate(shifted + [rim_part], axis=2).transpose(1, 0, 2)
    span = windows.shape[2]
    position = jnp.arange(width, dtype=jnp.int32)
    anchor = position // block_len * block_len
    column = jnp.where(
        neighbours < slots,
        neighbours - anchor[None, :] + 64,
        jnp.where(neighbours < slots + 2 * rim, pieces * block_len + neighbours - slots, -1),
    )
    column = column.reshape(neighbours.shape[0], block_count, block_len).transpose(1, 0, 2)
    group_len = pick_group(block_count)
    windows = windows.reshape(block_count // group_len, group_len, lanes, span)
    column = column.reshape(block_count // group_len, group_len, neighbours.shape[0], block_len)

    def gather_block(item):
        window_set, column_set = item
        target = jnp.arange(span, dtype=jnp.int32)[None, None, :, None]
        hits = jnp.sum((column_set[:, :, None, :] == target).astype(jnp.float32), axis=1)
        return jnp.einsum("grw,gwb->grb", window_set, hits, precision=lax.Precision.HIGHEST)

    sums = lax.map(gather_block, (windows, column))
    sums = sums.reshape(block_count, lanes, block_len).transpose(1, 0, 2).reshape(lanes, width)
    coupling = masked_f * sums[-1][None, :] - sums[:-1]
    return weight[None] * weight[None] * masked_f + weight[None] * coupling


def on_device(sensitivity, direction, depth_weight, counts, send_lists, neighbours):
    slots = sensitivity.shape[1]
    nvecs = direction.shape[0]
    live = jnp.arange(slots, dtype=jnp.int32) < counts[0]
    masked = jnp.where(live[None, :], direction, jnp.zeros_like(direction))
    partial_data = lax.dot_general(
        masked, sensitivity, (((1,), (1,)), ((), ())), preferred_element_type=jnp.float32
    )
    summed = lax.psum(partial_data, "cell")
    rounded = summed.astype(jnp.bfloat16)
    remainder = (summed - rounded.astype(jnp.float32)).astype(jnp.bfloat16)
    stacked = jnp.concatenate([rounded, remainder], axis=0)
    both = jnp.dot(stacked, sensitivity, preferred_element_type=jnp.float32)
    partial_cells = both[:nvecs] + both[nvecs:]
    weight = jnp.where(live, depth_weight, jnp.float32(0.0))
    masked_f = masked.astype(jnp.float32)
    misfit = lax.psum(partial_cells, "dp")
    smooth = smoothness(masked_f, weight, send_lists, neighbours, slots)
    total = misfit + 0.5 * smooth
    return jnp.where(live[None, :], total, jnp.float32(0.0))


def solution(mesh):
    placed = (
        P("dp", "cell"),
        P(None, "cell"),
        P("cell"),
        P("cell"),
        P("cell", None, None),
        P(None, "cell"),
    )
    return jax.shard_map(
        on_device, mesh=mesh, in_specs=placed, out_specs=P(None, "cell"), check_vma=False
    )
```

profile of v0, /device:TPU:1, one launch (start us, length us, event | category | flops | bytes accessed | tf_op | source)
XLA Modules:
  0.0 220.8 jit_solution(9854497497350042663)
XLA Ops:
  7.3 0.8 fusion.22
  8.1 1.0 convert_multiply_fusion.1
  9.1 0.1 pad_maximum_fusion.1
  9.2 2.3 %copy.26 = f32[17,6272]{0,1:T(8,128)} copy(f32[17,6272]{1,0:T(8,128)S(1)} %pad_maximum_fusion.1) | data formatting | bytes 852992 | tf_op jit(solution)/shard_map/concatenate | solution.py:38
  11.6 2.6 %gather_fusion = f32[256,17]{1,0:T(8,128)S(1)} fusion(f32[17,6272]{0,1:T(8,128)} %copy.26, s32[1024]{0:T(1024)S(1)} %pad_clamp_fusion), kind=kCustom, calls=%fused_computation | custom fusion | bytes 35840 | tf_op jit(solution)/shard_map/jit(_take)/gather | solution.py:39
  14.2 0.1 select_bitcast_fusion
  14.3 0.7 fusion.23
  14.9 5.4 %collective-permute-start = (f32[17,128]{0,1:T(8,128)}, f32[17,128]{0,1:T(8,128)}, u32[]{:S(2)}, u32[]{:S(2)}) collective-permute-start(f32[17,128]{0,1:T(8,128)} %get-tuple-element.42), channel_id=1, source_target_pairs={{0,1},{1,2},{2,3},{3,4},{4,5},{5,6},{6,7},{7,8},{8,9},{9,10},{10,1... | collective-permute-start | bytes 26120 | tf_op jit(solution)/shard_map/ppermute | solution.py:14
  20.4 1.3 collective-permute-start.1
  21.7 0.5 fusion.10
  22.2 67.6 %psum.14 = f32[16,128]{1,0:T(8,128)S(1)} all-reduce(f32[16,128]{1,0:T(8,128)S(1)} %fusion.10), channel_id=1, replica_groups=mesh['dp'=16,'cell'=32] {'cell'}, use_global_device_ids=true, to_apply=%region_0.1 | all-reduce | flops 2048 | bytes 16384 | tf_op jit(solution)/shard_map/psum | solution.py:90
  89.8 0.4 fusion.16
  90.1 0.8 slice_add_fusion
  91.0 0.7 select_select_fusion
  91.7 0.4 pad_slice_fusion.1
  92.1 0.8 reshape.80
  92.9 1.1 copy.29
  94.1 0.1 reshape.81
  94.1 0.1 copy.30
  94.2 0.9 copy.27
  95.2 0.1 copy.28
  95.3 0.1 broadcast_in_dim.71
  95.4 1.7 pad_maximum_fusion
  97.1 30.0 %while.10 = (s32[]{:T(128)}, f32[7,7,17,128]{3,2,1,0:T(8,128)S(1)}, f32[7,7,17,512]{3,2,1,0:T(8,128)}, s32[7,7,6,128]{3,2,1,0:T(8,128)}, s32[]{:T(128)}) while((s32[]{:T(128)}, f32[7,7,17,128]{3,2,1,0:T(8,128)S(1)}, f32[7,7,17,512]{3,2,1,0:T(8,128)}, s32[7,7,6,128]{3,2,1,0:T(8,128)}, s32[]{:T(128)}) %tuple.29), condition=%wide.region_4.5_spmd, body=%wide.region_2.4_spmd.sunk | while | flops 101384192 | bytes 4165697 | solution.py:76
  97.1 0.8 dynamic-slice_bitcast_fusion.2
  97.9 1.5 convert_reduce_fusion.2
  99.4 2.0 fusion.32
  101.4 0.8 dynamic-slice_bitcast_fusion.2
  102.2 1.5 convert_reduce_fusion.2
  103.7 2.0 fusion.32
  105.7 0.8 dynamic-slice_bitcast_fusion.2
  106.5 1.5 convert_reduce_fusion.2
  107.9 2.0 fusion.32
  110.0 0.8 dynamic-slice_bitcast_fusion.2
  110.8 1.5 convert_reduce_fusion.2
  112.2 2.0 fusion.32
  114.3 0.8 dynamic-slice_bitcast_fusion.2
  115.0 1.5 convert_reduce_fusion.2
  116.5 2.0 fusion.32
  118.6 0.8 dynamic-slice_bitcast_fusion.2
  119.3 1.5 convert_reduce_fusion.2
  120.8 2.0 fusion.32
  122.8 0.8 dynamic-slice_bitcast_fusion.2
  123.6 1.5 convert_reduce_fusion.2
  125.1 2.0 fusion.32
  127.1 0.1 copy.36
  127.3 84.8 %all-reduce.3.cloned.1.call-done = f32[16,6272]{1,0:T(8,128)} async-done(((f32[16,6272]{1,0:T(8,128)}), f32[16,6272]{1,0:T(8,128)}) %all-reduce.3.cloned.1.call-update) | async-done | bytes 401424 | tf_op jit(solution)/shard_map/psum | solution.py:98
  212.1 1.9 fusion.7
  (27 shorter events, 0.2 us)
Async XLA Ops:
  6.5 15.1 %copy-start = (bf16[128,6272]{1,0:T(8,128)(2,1)S(1)}, bf16[128,6272]{1,0:T(8,128)(2,1)}, u32[]{:S(2)}) copy-start(bf16[128,6272]{1,0:T(8,128)(2,1)} %param.8) | copy-start | bytes 4816900
  6.5 205.5 %all-reduce.3.cloned.1.call-start = ((), (), s32[]{:S(2)}) async-start(), calls=%async_computation | async-start | bytes 802816 | tf_op jit(solution)/shard_map/psum | solution.py:98
  9.1 2.4 %copy-start.5 = (s32[1,2,128]{2,1,0:T(2,128)S(1)}, s32[1,2,128]{2,1,0:T(2,128)}, u32[]{:S(2)}) copy-start(s32[1,2,128]{2,1,0:T(2,128)} %param.12) | copy-start | bytes 3076
  9.2 12.5 %copy-start.1 = (bf16[16,6272]{1,0:T(8,128)(2,1)S(1)}, bf16[16,6272]{1,0:T(8,128)(2,1)}, u32[]{:S(2)}) copy-start(bf16[16,6272]{1,0:T(8,128)(2,1)} %param.9) | copy-start | bytes 602116
  14.9 79.3 %collective-permute-start = (f32[17,128]{0,1:T(8,128)}, f32[17,128]{0,1:T(8,128)}, u32[]{:S(2)}, u32[]{:S(2)}) collective-permute-start(f32[17,128]{0,1:T(8,128)} %get-tuple-element.42), channel_id=1, source_target_pairs={{0,1},{1,2},{2,3},{3,4},{4,5},{5,6},{6,7},{7,8},{8,9},{9,10},{10,1... | collective-permute-start | bytes 26120 | tf_op jit(solution)/shard_map/ppermute | solution.py:14
  20.4 74.8 %collective-permute-start.1 = (f32[17,128]{0,1:T(8,128)}, f32[17,128]{0,1:T(8,128)S(1)}, u32[]{:S(2)}, u32[]{:S(2)}) collective-permute-start(f32[17,128]{0,1:T(8,128)} %get-tuple-element.43), channel_id=1, source_target_pairs={{1,0},{2,1},{3,2},{4,3},{5,4},{6,5},{7,6},{8,7},{9,8},{10,9},{11,1... | collective-permute-start | bytes 26120 | tf_op jit(solution)/shard_map/ppermute | solution.py:15
  22.2 68.8 %copy-start.4 = (s32[6,6272]{1,0:T(8,128)S(1)}, s32[6,6272]{1,0:T(8,128)}, u32[]{:S(2)}) copy-start(s32[6,6272]{1,0:T(8,128)} %param.13) | copy-start | bytes 451588
  95.4 1.8 copy-start.3
  97.1 115.0 %copy-start.2 = (bf16[16,6272]{1,0:T(8,128)(2,1)S(1)}, bf16[16,6272]{1,0:T(8,128)(2,1)}, u32[]{:S(2)}) copy-start(bf16[16,6272]{1,0:T(8,128)(2,1)} %param.9) | copy-start | bytes 602116
Sparse Core Ops, SparseCore 0:
  91.1 120.9 all-reduce.2
where the time goes:
time: 222 us; the launch traced here: 221 us
  waiting for transfers between devices  84.8 us (38%)
  blocking collectives  67.6 us (30%)
  other arithmetic  17.4 us (8%)
  matrix products  15 us (7%)
  local copies, waits for them, and re-layouts  14.7 us (7%)
  between operations  14.4 us (6%)
  starting transfers between devices  6.7 us (3%)
    psum x1, waiting for transfers between devices, on_device(): misfit = lax.psum(partial_cells, 'dp')  84.8 us
    psum x1, blocking collectives, on_device(): summed = lax.psum(partial_data, 'cell')  67.6 us
    dot_general x7, matrix products, gather_block(): jnp.einsum('grw,gwb->grb', window_set, hits, precision=lax.Precision.HIGH...  14.2 us
    reduce_sum x7, other arithmetic, gather_block(): jnp.sum((column_set[:, :, None, :] == target).astype(jnp.float32), axis=1)  10.3 us
    ppermute x1, starting transfers between devices, padded_2(): before = lax.ppermute(last, axis, up)  5.42 us
    eq x7, local copies, waits for them, and re-layouts, gather_block(): column_set[:, :, None, :] == target  5.32 us
  transfers between devices with their start and end apart: 3, of which 1 were waited for; matrix products, arithmetic and copies ran while one was open for 17% of the time, Pallas kernels for 0%

commit v1 on v0

--- a/solution.py
+++ b/solution.py
@@ -95,7 +95,7 @@
     partial_cells = both[:nvecs] + both[nvecs:]
     weight = jnp.where(live, depth_weight, jnp.float32(0.0))
     masked_f = masked.astype(jnp.float32)
-    misfit = lax.psum(partial_cells, "dp")
+    misfit = jnp.sum(lax.all_gather(partial_cells, "dp"), axis=0)
     smooth = smoothness(masked_f, weight, send_lists, neighbours, slots)
     total = misfit + 0.5 * smooth
     return jnp.where(live[None, :], total, jnp.float32(0.0))

time: 222 us -> 153 us (0.69)
  the two profiles are of different devices: /device:TPU:1 before, /device:TPU:32 now
where the time goes in v1:
time: 153 us; the launch traced here: 152 us
  blocking collectives  82 us (54%)
  other arithmetic  18 us (12%)
  matrix products  16 us (10%)
  local copies, waits for them, and re-layouts  15.4 us (10%)
  between operations  14.4 us (9%)
  starting transfers between devices  5.83 us (4%)
    psum x1, blocking collectives, on_device(): summed = lax.psum(partial_data, 'cell')  82 us
    dot_general x7, matrix products, gather_block(): jnp.einsum('grw,gwb->grb', window_set, hits, precision=lax.Precision.HIGH...  14.2 us
    reduce_sum x7, other arithmetic, gather_block(): jnp.sum((column_set[:, :, None, :] == target).astype(jnp.float32), axis=1)  10.3 us
    eq x7, local copies, waits for them, and re-layouts, gather_block(): column_set[:, :, None, :] == target  5.3 us
    ppermute x1, starting transfers between devices, padded_2(): before = lax.ppermute(last, axis, up)  4.55 us
    reduce_sum x1, other arithmetic, on_device(): misfit = jnp.sum(lax.all_gather(partial_cells, 'dp'), axis=0)  3.23 us
  transfers between devices with their start and end apart: 3, of which 0 were waited for; matrix products, arithmetic and copies ran while one was open for 28% of the time, Pallas kernels for 0%

profile of v1, /device:TPU:32, one launch (start us, length us, event | category | flops | bytes accessed | tf_op | source)
XLA Modules:
  0.0 152.0 jit_solution(8363669606918623620)
XLA Ops:
  7.3 0.6 copy-done
  8.0 1.4 fusion.10
  9.4 82.0 %psum.7 = f32[16,128]{1,0:T(8,128)S(1)} all-reduce(f32[16,128]{1,0:T(8,128)S(1)} %fusion.10), channel_id=1, replica_groups=mesh['dp'=16,'cell'=32] {'cell'}, use_global_device_ids=true, to_apply=%region_0.1 | all-reduce | flops 2048 | bytes 16384 | tf_op jit(solution)/shard_map/psum | solution.py:90
  91.5 0.4 fusion.16
  91.8 0.8 slice_add_fusion
  92.7 0.1 convert_multiply_fusion.1
  92.8 0.1 pad_maximum_fusion.1
  92.9 2.4 %copy.37 = f32[17,6272]{0,1:T(8,128)} copy(f32[17,6272]{1,0:T(8,128)S(1)} %pad_maximum_fusion.1) | data formatting | bytes 852992 | tf_op jit(solution)/shard_map/concatenate | solution.py:38
  95.3 2.6 %gather_fusion = f32[256,17]{1,0:T(8,128)S(1)} fusion(f32[17,6272]{0,1:T(8,128)} %copy.37, s32[1024]{0:T(1024)S(1)} %pad_clamp_fusion), kind=kCustom, calls=%fused_computation | custom fusion | bytes 35840 | tf_op jit(solution)/shard_map/jit(_take)/gather | solution.py:39
  97.9 0.1 select_bitcast_fusion
  98.1 0.7 fusion.23
  98.7 1.3 collective-permute-start.1
  100.0 4.5 %collective-permute-start = (f32[17,128]{0,1:T(8,128)}, f32[17,128]{0,1:T(8,128)S(1)}, u32[]{:S(2)}, u32[]{:S(2)}) collective-permute-start(f32[17,128]{0,1:T(8,128)} %get-tuple-element.42), channel_id=1, source_target_pairs={{0,1},{1,2},{2,3},{3,4},{4,5},{5,6},{6,7},{7,8},{8,9},{9,10},{10,1... | collective-permute-start | bytes 26120 | tf_op jit(solution)/shard_map/ppermute | solution.py:14
  104.6 0.7 select_select_fusion
  105.3 0.4 pad_slice_fusion.1
  105.7 0.8 reshape.81
  106.5 1.1 copy.41
  107.7 0.1 reshape.80
  107.7 0.1 copy.40
  107.9 0.9 copy.39
  108.8 0.1 copy.38
  108.9 0.1 broadcast_in_dim.71
  109.0 1.8 %pad_maximum_fusion = f32[17,49,512]{2,0,1:T(8,128)} fusion(f32[17,49,256]{2,0,1:T(8,128)S(1)} %broadcast_in_dim.71, f32[17,49,128]{2,0,1:T(8,128)S(1)} %copy.41, f32[17,49,128]{2,0,1:T(8,128)S(1)} %copy.40), kind=kLoop, calls=%fused_computation.9 | loop fusion | flops 852992 | bytes 3411968 | tf_op jit(solution)/shard_map/concatenate | solution.py:56
  110.8 30.0 %while.10 = (s32[]{:T(128)}, f32[7,7,17,128]{3,2,1,0:T(8,128)S(1)}, f32[7,7,17,512]{3,2,1,0:T(8,128)}, s32[7,7,6,128]{3,2,1,0:T(8,128)}, s32[]{:T(128)}) while((s32[]{:T(128)}, f32[7,7,17,128]{3,2,1,0:T(8,128)S(1)}, f32[7,7,17,512]{3,2,1,0:T(8,128)}, s32[7,7,6,128]{3,2,1,0:T(8,128)}, s32[]{:T(128)}) %tuple.29), condition=%wide.region_4.5_spmd, body=%wide.region_2.4_spmd.sunk | while | flops 101384192 | bytes 4165705 | solution.py:76
  110.8 0.8 dynamic-slice_bitcast_fusion.2
  111.5 1.5 convert_reduce_fusion.2
  113.0 2.0 %fusion.32 = f32[7,7,17,128]{3,2,1,0:T(8,128)S(1)} fusion(f32[7,7,17,128]{3,2,1,0:T(8,128)S(1)} %get-tuple-element.75, s32[]{:T(128)S(6)} %copy.52, f32[7,512,128]{2,1,0:T(8,128)S(1)} %convert_reduce_fusion.2, f32[7,7,17,512]{3,2,1,0:T(8,128)} %get-tuple-element.81), kind=kOutput, calls=%fused_computation.4.clone.1 | convolution fusion | flops 93585408 | bytes 2266112 | tf_op jit(solution)/shard_map/while/body/eval_jaxpr/grw,gwb->grb/dot_general | solution.py:74
  115.0 0.8 dynamic-slice_bitcast_fusion.2
  115.8 1.5 convert_reduce_fusion.2
  117.3 2.0 %fusion.32 = f32[7,7,17,128]{3,2,1,0:T(8,128)S(1)} fusion(f32[7,7,17,128]{3,2,1,0:T(8,128)S(1)} %get-tuple-element.75, s32[]{:T(128)S(6)} %copy.52, f32[7,512,128]{2,1,0:T(8,128)S(1)} %convert_reduce_fusion.2, f32[7,7,17,512]{3,2,1,0:T(8,128)} %get-tuple-element.81), kind=kOutput, calls=%fused_computation.4.clone.1 | convolution fusion | flops 93585408 | bytes 2266112 | tf_op jit(solution)/shard_map/while/body/eval_jaxpr/grw,gwb->grb/dot_general | solution.py:74
  119.3 0.8 dynamic-slice_bitcast_fusion.2
  120.1 1.5 convert_reduce_fusion.2
  121.6 2.0 %fusion.32 = f32[7,7,17,128]{3,2,1,0:T(8,128)S(1)} fusion(f32[7,7,17,128]{3,2,1,0:T(8,128)S(1)} %get-tuple-element.75, s32[]{:T(128)S(6)} %copy.52, f32[7,512,128]{2,1,0:T(8,128)S(1)} %convert_reduce_fusion.2, f32[7,7,17,512]{3,2,1,0:T(8,128)} %get-tuple-element.81), kind=kOutput, calls=%fused_computation.4.clone.1 | convolution fusion | flops 93585408 | bytes 2266112 | tf_op jit(solution)/shard_map/while/body/eval_jaxpr/grw,gwb->grb/dot_general | solution.py:74
  123.6 0.8 dynamic-slice_bitcast_fusion.2
  124.4 1.5 convert_reduce_fusion.2
  125.9 2.0 %fusion.32 = f32[7,7,17,128]{3,2,1,0:T(8,128)S(1)} fusion(f32[7,7,17,128]{3,2,1,0:T(8,128)S(1)} %get-tuple-element.75, s32[]{:T(128)S(6)} %copy.52, f32[7,512,128]{2,1,0:T(8,128)S(1)} %convert_reduce_fusion.2, f32[7,7,17,512]{3,2,1,0:T(8,128)} %get-tuple-element.81), kind=kOutput, calls=%fused_computation.4.clone.1 | convolution fusion | flops 93585408 | bytes 2266112 | tf_op jit(solution)/shard_map/while/body/eval_jaxpr/grw,gwb->grb/dot_general | solution.py:74
  127.9 0.8 dynamic-slice_bitcast_fusion.2
  128.7 1.5 convert_reduce_fusion.2
  130.2 2.0 %fusion.32 = f32[7,7,17,128]{3,2,1,0:T(8,128)S(1)} fusion(f32[7,7,17,128]{3,2,1,0:T(8,128)S(1)} %get-tuple-element.75, s32[]{:T(128)S(6)} %copy.52, f32[7,512,128]{2,1,0:T(8,128)S(1)} %convert_reduce_fusion.2, f32[7,7,17,512]{3,2,1,0:T(8,128)} %get-tuple-element.81), kind=kOutput, calls=%fused_computation.4.clone.1 | convolution fusion | flops 93585408 | bytes 2266112 | tf_op jit(solution)/shard_map/while/body/eval_jaxpr/grw,gwb->grb/dot_general | solution.py:74
  132.2 0.8 dynamic-slice_bitcast_fusion.2
  133.0 1.5 convert_reduce_fusion.2
  134.4 2.0 %fusion.32 = f32[7,7,17,128]{3,2,1,0:T(8,128)S(1)} fusion(f32[7,7,17,128]{3,2,1,0:T(8,128)S(1)} %get-tuple-element.75, s32[]{:T(128)S(6)} %copy.52, f32[7,512,128]{2,1,0:T(8,128)S(1)} %convert_reduce_fusion.2, f32[7,7,17,512]{3,2,1,0:T(8,128)} %get-tuple-element.81), kind=kOutput, calls=%fused_computation.4.clone.1 | convolution fusion | flops 93585408 | bytes 2266112 | tf_op jit(solution)/shard_map/while/body/eval_jaxpr/grw,gwb->grb/dot_general | solution.py:74
  136.5 0.8 dynamic-slice_bitcast_fusion.2
  137.2 1.5 convert_reduce_fusion.2
  138.7 2.0 %fusion.32 = f32[7,7,17,128]{3,2,1,0:T(8,128)S(1)} fusion(f32[7,7,17,128]{3,2,1,0:T(8,128)S(1)} %get-tuple-element.75, s32[]{:T(128)S(6)} %copy.52, f32[7,512,128]{2,1,0:T(8,128)S(1)} %convert_reduce_fusion.2, f32[7,7,17,512]{3,2,1,0:T(8,128)} %get-tuple-element.81), kind=kOutput, calls=%fused_computation.4.clone.1 | convolution fusion | flops 93585408 | bytes 2266112 | tf_op jit(solution)/shard_map/while/body/eval_jaxpr/grw,gwb->grb/dot_general | solution.py:74
  140.8 0.1 copy.48
  141.0 3.2 %reduce_sum.18 = f32[16,6272]{1,0:T(8,128)S(1)} reduce(f32[16,16,6272]{2,1,0:T(8,128)} %bitcast.48, f32[]{:T(128)} %constant.53.clone.1), dimensions={0}, to_apply=%region_1.2 | reduce | flops 1505280 | bytes 6823940 | tf_op jit(solution)/shard_map/reduce_sum | solution.py:98
  144.2 0.9 fusion.7
  (30 shorter events, 0.2 us)
Async XLA Ops:
  6.5 1.4 copy-start
  6.5 134.4 %all-gather.3.cloned.1.call-start = ((), (), s32[]{:S(2)}) async-start(), calls=%async_computation | async-start | bytes 6823936 | tf_op jit(solution)/shard_map/all_gather | solution.py:98
  9.4 83.3 %copy-start.5 = (f32[6272]{0:T(1024)S(1)}, f32[6272]{0:T(1024)}, u32[]{:S(2)}) copy-start(f32[6272]{0:T(1024)} %param.10) | copy-start | bytes 75268
  9.4 83.3 %copy-start.1 = (bf16[16,6272]{1,0:T(8,128)(2,1)S(1)}, bf16[16,6272]{1,0:T(8,128)(2,1)}, u32[]{:S(2)}) copy-start(bf16[16,6272]{1,0:T(8,128)(2,1)} %param.9) | copy-start | bytes 602116
  92.8 2.5 %copy-start.6 = (s32[1,2,128]{2,1,0:T(2,128)S(1)}, s32[1,2,128]{2,1,0:T(2,128)}, u32[]{:S(2)}) copy-start(s32[1,2,128]{2,1,0:T(2,128)} %param.12) | copy-start | bytes 3076
  92.8 11.7 %copy-start.4 = (s32[6,6272]{1,0:T(8,128)S(1)}, s32[6,6272]{1,0:T(8,128)}, u32[]{:S(2)}) copy-start(s32[6,6272]{1,0:T(8,128)} %param.13) | copy-start | bytes 451588
  98.7 9.2 %collective-permute-start.1 = (f32[17,128]{0,1:T(8,128)}, f32[17,128]{0,1:T(8,128)}, u32[]{:S(2)}, u32[]{:S(2)}) collective-permute-start(f32[17,128]{0,1:T(8,128)} %get-tuple-element.43), channel_id=1, source_target_pairs={{1,0},{2,1},{3,2},{4,3},{5,4},{6,5},{7,6},{8,7},{9,8},{10,9},{11,1... | collective-permute-start | bytes 26120 | tf_op jit(solution)/shard_map/ppermute | solution.py:15
  100.0 8.8 %collective-permute-start = (f32[17,128]{0,1:T(8,128)}, f32[17,128]{0,1:T(8,128)S(1)}, u32[]{:S(2)}, u32[]{:S(2)}) collective-permute-start(f32[17,128]{0,1:T(8,128)} %get-tuple-element.42), channel_id=1, source_target_pairs={{0,1},{1,2},{2,3},{3,4},{4,5},{5,6},{6,7},{7,8},{8,9},{9,10},{10,1... | collective-permute-start | bytes 26120 | tf_op jit(solution)/shard_map/ppermute | solution.py:14
  109.0 1.8 %copy-start.3 = (f32[7,7,17,128]{3,2,1,0:T(8,128)S(1)}, f32[7,7,17,128]{3,2,1,0:T(8,128)}, u32[]{:S(2)}) copy-start(f32[7,7,17,128]{3,2,1,0:T(8,128)} %custom-call.2) | copy-start | bytes 1279492
  140.9 3.2 %copy-start.2 = (bf16[16,6272]{1,0:T(8,128)(2,1)S(1)}, bf16[16,6272]{1,0:T(8,128)(2,1)}, u32[]{:S(2)}) copy-start(bf16[16,6272]{1,0:T(8,128)(2,1)} %param.9) | copy-start | bytes 602116
Sparse Core Ops, SparseCore 0:
  92.8 40.0 all-gather.2
